TPU v7x, 256 devices: a whole 4x4x8 slice. The times are simulated.
256 devices in a mesh: dom: 32 (over y_hi, z, core), tp: 8 (over x, y_lo).
Axes of the slice: x: 4, y: 4 (y_hi: 2, y_lo: 2; y = y_hi * 2 + y_lo), z: 8, core: 2. Of those that a mesh axis runs over, the one named last changes fastest.
Arguments:
- hidden_in: bfloat16 [448, 64, 4096], P('dom', None, 'tp'), may hold values from -6 to 6
- query_weight: bfloat16 [4096, 4096], P('dom', 'tp'), may hold values from -0.09375 to 0.09375
- segment_keys: bfloat16 [448, 64, 1024], P('dom', None, 'tp'), may hold values from -6 to 6
- segment_values: bfloat16 [448, 64, 1024], P('dom', None, 'tp'), may hold values from -6 to 6
- prefix_keys: bfloat16 [32, 256, 1024], P('dom', None, 'tp'), may hold values from -80 to 80
- prefix_values: bfloat16 [32, 256, 1024], P('dom', None, 'tp'), may hold values from -6 to 6
- ancestors: int32 [448], P('dom'), may hold values from 0 to 31, as said below
- twist_weights: float32 [448], P('dom'), may hold values from 0.25 to 4
- out_grad: bfloat16 [448, 64, 4096], P('dom', None, 'tp'), may hold values from -24 to 24
Outputs:
- grad_query_weight: bfloat16 [4096, 4096], P('dom', 'tp')
- grad_segment_keys: bfloat16 [448, 64, 1024], P('dom', None, 'tp')
- grad_segment_values: bfloat16 [448, 64, 1024], P('dom', None, 'tp')
- grad_prefix_keys: float32 [32, 256, 1024], P('dom', None, 'tp')
- grad_prefix_values: float32 [32, 256, 1024], P('dom', None, 'tp')
Inputs may be any that keep to these rules, and one draw needn't show every extreme that they name: `ancestors`: among the 14 consecutive particles of one device, no ancestor is named more than 2 times, and one ancestor, the same for all devices, is named exactly 2 times on every device.
All inputs are finite; a program needn't handle non-finite values.
Results may differ from a plain program's by a relative error of at most 0.02.
The roundings to bfloat16 on the way count: a program that leaves them out, or rounds other values in their place, can miss the bound.
Values may be sent and summed in bfloat16 or wider, within the bound.
No kernel may reach another device: no remote copies, remote signals or barrier semaphores. Data moves between devices by JAX's collectives and lax.ppermute only.
A program may use at most 128 MiB of HBM per device.

v0:
```python
import math
import jax
import jax.numpy as jnp
from jax import lax
from jax.sharding import PartitionSpec as P

HD = 128


def attend(queries, scaled, seg_keys, seg_values, pre_keys, pre_values):
    factor = 1.0 / math.sqrt(queries.shape[-1])
    score_pre = (
        jnp.einsum("bikgd,bjkd->bkgij", queries, pre_keys, preferred_element_type=jnp.float32)
        * factor
    )
    score_seg = (
        jnp.einsum("bikgd,bjkd->bkgij", queries, seg_keys, preferred_element_type=jnp.float32)
        * factor
    )
    length = queries.shape[1]
    causal = lax.broadcasted_iota(jnp.int32, (length, length), 0) >= lax.broadcasted_iota(
        jnp.int32, (length, length), 1
    )
    score_seg = jnp.where(causal, score_seg, -jnp.inf)
    row_max = jnp.maximum(jnp.max(score_pre, -1), jnp.max(score_seg, -1))[..., None]
    exp_pre = jnp.exp(score_pre - row_max)
    exp_seg = jnp.exp(score_seg - row_max)
    denominator = (jnp.sum(exp_pre, -1) + jnp.sum(exp_seg, -1))[..., None]
    prob_pre = exp_pre / denominator
    prob_seg = exp_seg / denominator
    dprob_pre = jnp.einsum(
        "bikgd,bjkd->bkgij", scaled, pre_values, preferred_element_type=jnp.float32
    )
    dprob_seg = jnp.einsum(
        "bikgd,bjkd->bkgij", scaled, seg_values, preferred_element_type=jnp.float32
    )
    row_delta = (jnp.sum(prob_pre * dprob_pre, -1) + jnp.sum(prob_seg * dprob_seg, -1))[..., None]
    dscore_pre = (prob_pre * (dprob_pre - row_delta)).astype(jnp.bfloat16)
    dscore_seg = (prob_seg * (dprob_seg - row_delta)).astype(jnp.bfloat16)
    grad_q = (
        jnp.einsum("bkgij,bjkd->bikgd", dscore_pre, pre_keys, preferred_element_type=jnp.float32)
        + jnp.einsum("bkgij,bjkd->bikgd", dscore_seg, seg_keys, preferred_element_type=jnp.float32)
    ) * factor
    grad_pk = (
        jnp.einsum("bkgij,bikgd->bjkd", dscore_pre, queries, preferred_element_type=jnp.float32)
        * factor
    )
    grad_pv = jnp.einsum(
        "bkgij,bikgd->bjkd",
        prob_pre.astype(jnp.bfloat16),
        scaled,
        preferred_element_type=jnp.float32,
    )
    grad_sk = (
        jnp.einsum("bkgij,bikgd->bjkd", dscore_seg, queries, preferred_element_type=jnp.float32)
        * factor
    )
    grad_sv = jnp.einsum(
        "bkgij,bikgd->bjkd",
        prob_seg.astype(jnp.bfloat16),
        scaled,
        preferred_element_type=jnp.float32,
    )
    return (
        grad_q.astype(jnp.bfloat16),
        grad_sk.astype(jnp.bfloat16),
        grad_sv.astype(jnp.bfloat16),
        grad_pk,
        grad_pv,
    )


def local(
    hidden_in,
    query_weight,
    segment_keys,
    segment_values,
    prefix_keys,
    prefix_values,
    ancestors,
    twist_weights,
    out_grad,
):
    particles_here = hidden_in.shape[0]
    length = hidden_in.shape[1]
    features = lax.all_gather(hidden_in, "tp", axis=2, tiled=True)
    token_rows = features.reshape(particles_here * length, features.shape[2])
    width_q = query_weight.shape[1]
    width_kv = segment_keys.shape[2]
    kv_heads = width_kv // HD
    group_size = width_q // width_kv
    prefix = prefix_keys.shape[1]
    columns = token_rows
    queries = jnp.dot(
        columns,
        lax.all_gather(query_weight, "dom", axis=0, tiled=True),
        preferred_element_type=jnp.float32,
    ).astype(jnp.bfloat16)
    queries = queries.reshape(particles_here, length, width_q)
    scaled = (out_grad.astype(jnp.float32) * twist_weights[:, None, None]).astype(jnp.bfloat16)
    owners = lax.axis_size("dom")
    capacity = max(2, (2 * particles_here + owners - 1) // owners)
    positions = jnp.arange(particles_here, dtype=jnp.int32)
    shared = ancestors[:, None] == ancestors[None, :]
    slot_rank = jnp.sum(
        (shared & (positions[:, None] > positions[None, :])).astype(jnp.int32), axis=1
    )
    owner_ids = jnp.arange(owners, dtype=jnp.int32)
    slot_ids = jnp.arange(capacity, dtype=jnp.int32)
    slot_table = (
        (ancestors[None, None, :] == owner_ids[:, None, None])
        & (slot_rank[None, None, :] == slot_ids[None, :, None])
    ).astype(jnp.bfloat16)

    def to_slots(block):
        return jnp.einsum(
            "acp,piw->aciw", slot_table, block, preferred_element_type=jnp.float32
        ).astype(jnp.bfloat16)

    def from_slots(block):
        return jnp.einsum(
            "acp,aciw->piw", slot_table, block, preferred_element_type=jnp.float32
        ).astype(jnp.bfloat16)

    arrived = (
        lax.all_to_all(to_slots(queries), "dom", split_axis=0, concat_axis=0, tiled=True),
        lax.all_to_all(to_slots(scaled), "dom", split_axis=0, concat_axis=0, tiled=True),
        lax.all_to_all(to_slots(segment_keys), "dom", split_axis=0, concat_axis=0, tiled=True),
        lax.all_to_all(to_slots(segment_values), "dom", split_axis=0, concat_axis=0, tiled=True),
    )
    sources = max(
        (
            divisor
            for divisor in range(1, owners + 1)
            if owners % divisor == 0 and divisor * capacity <= max(particles_here, capacity)
        )
    )
    block_count = owners // sources
    slot_count = sources * capacity
    own_keys = jnp.broadcast_to(
        prefix_keys.reshape(1, prefix, kv_heads, HD), (slot_count, prefix, kv_heads, HD)
    )
    own_values = jnp.broadcast_to(
        prefix_values.reshape(1, prefix, kv_heads, HD), (slot_count, prefix, kv_heads, HD)
    )

    def handle(carried, entry):
        slot_q, slot_o, slot_k, slot_v = entry
        grad_q, grad_sk, grad_sv, grad_pk, grad_pv = attend(
            slot_q.reshape(slot_count, length, kv_heads, group_size, HD),
            slot_o.reshape(slot_count, length, kv_heads, group_size, HD),
            slot_k.reshape(slot_count, length, kv_heads, HD),
            slot_v.reshape(slot_count, length, kv_heads, HD),
            own_keys,
            own_values,
        )
        updated = (carried[0] + jnp.sum(grad_pk, 0), carried[1] + jnp.sum(grad_pv, 0))
        return (
            updated,
            (
                grad_q.reshape(slot_count, length, width_q),
                grad_sk.reshape(slot_count, length, width_kv),
                grad_sv.reshape(slot_count, length, width_kv),
            ),
        )

    blocks = tuple(
        (member.reshape(block_count, slot_count, length, member.shape[-1]) for member in arrived)
    )
    nothing = jnp.zeros((prefix, kv_heads, HD), jnp.float32)
    (sum_keys, sum_values), (out_q, out_k, out_v) = lax.scan(handle, (nothing, nothing), blocks)
    returned = (
        lax.all_to_all(
            out_q.reshape(owners, capacity, length, width_q),
            "dom",
            split_axis=0,
            concat_axis=0,
            tiled=True,
        ),
        lax.all_to_all(
            out_k.reshape(owners, capacity, length, width_kv),
            "dom",
            split_axis=0,
            concat_axis=0,
            tiled=True,
        ),
        lax.all_to_all(
            out_v.reshape(owners, capacity, length, width_kv),
            "dom",
            split_axis=0,
            concat_axis=0,
            tiled=True,
        ),
    )
    grad_queries = from_slots(returned[0])
    grad_seg_keys = from_slots(returned[1])
    grad_seg_values = from_slots(returned[2])
    grad_pre_keys = sum_keys.reshape(1, prefix, width_kv)
    grad_pre_values = sum_values.reshape(1, prefix, width_kv)
    grad_rows = grad_queries.reshape(particles_here * length, width_q)
    columns = token_rows
    grad_weight = lax.psum_scatter(
        jnp.einsum("tc,tq->cq", columns, grad_rows, preferred_element_type=jnp.float32).astype(
            jnp.bfloat16
        ),
        "dom",
        scatter_dimension=0,
        tiled=True,
    )
    return (grad_weight, grad_seg_keys, grad_seg_values, grad_pre_keys, grad_pre_values)


def solution(mesh):
    return jax.shard_map(
        local,
        mesh=mesh,
        in_specs=(
            P("dom", None, "tp"),
            P("dom", "tp"),
            P("dom", None, "tp"),
            P("dom", None, "tp"),
            P("dom", None, "tp"),
            P("dom", None, "tp"),
            P("dom"),
            P("dom"),
            P("dom", None, "tp"),
        ),
        out_specs=(
            P("dom", "tp"),
            P("dom", None, "tp"),
            P("dom", None, "tp"),
            P("dom", None, "tp"),
            P("dom", None, "tp"),
        ),
        check_vma=False,
    )
```

profile of v0, /device:TPU:2, one launch (start us, length us, event | category | flops | bytes accessed | tf_op | source)
XLA Modules:
  0.0 876.4 jit_solution(134274365021562520)
XLA Ops:
  13.3 11.6 %all-to-all-start.3 = ((bf16[32,2,64,128]{3,2,1,0:T(8,128)(2,1)}), bf16[32,2,64,128]{3,2,1,0:T(8,128)(2,1)S(1)}, u32[]{:S(2)}, u32[]{:S(2)}) async-start(bf16[32,2,64,128]{3,2,1,0:T(8,128)(2,1)} %copy.158), calls=%async_computation.3 | async-start | bytes 2097152 | tf_op jit(solution)/shard_map/all_to_all | solution.py:129
  26.9 32.4 %all-to-all-done.3 = bf16[32,2,64,128]{3,2,1,0:T(8,128)(2,1)S(1)} async-done(((bf16[32,2,64,128]{3,2,1,0:T(8,128)(2,1)}), bf16[32,2,64,128]{3,2,1,0:T(8,128)(2,1)S(1)}, u32[]{:S(2)}, u32[]{:S(2)}) %all-to-all-start.3) | async-done | bytes 1048608 | tf_op jit(solution)/shard_map/all_to_all | solution.py:129
  59.3 4.7 all-to-all-start.1
  65.6 4.4 copy.156
  70.0 27.1 %all-to-all-done.1 = bf16[32,2,64,128]{3,2,1,0:T(8,128)(2,1)} async-done(((bf16[32,2,64,128]{3,2,1,0:T(8,128)(2,1)}), bf16[32,2,64,128]{3,2,1,0:T(8,128)(2,1)}, u32[]{:S(2)}, u32[]{:S(2)}) %all-to-all-start.1) | async-done | bytes 1048608 | tf_op jit(solution)/shard_map/all_to_all | solution.py:128
  97.1 5.4 all-to-all-start.2
  102.6 21.5 %all-gather.5.cloned.1.call-done = bf16[4096,512]{1,0:T(8,128)(2,1)} async-done(((bf16[128,512]{1,0:T(8,128)(2,1)}), bf16[4096,512]{1,0:T(8,128)(2,1)}) %all-gather.5.cloned.1.call-update) | async-done | bytes 4194320 | tf_op jit(solution)/shard_map/all_gather | solution.py:96
  124.0 178.3 %all-gather.3.cloned.1.call-done = bf16[14,64,4096]{2,1,0:T(8,128)(2,1)} async-done(((bf16[14,64,512]{2,1,0:T(8,128)(2,1)}), bf16[14,64,4096]{2,1,0:T(8,128)(2,1)}) %all-gather.3.cloned.1.call-update) | async-done | bytes 7340048 | tf_op jit(solution)/shard_map/all_gather | solution.py:86
  302.3 8.2 convolution_convert_fusion.4
  311.9 4.4 copy.152
  316.3 8.2 all-to-all-start
  324.8 96.4 %all-to-all-done = bf16[32,2,64,512]{3,2,1,0:T(8,128)(2,1)} async-done(((bf16[32,2,64,512]{3,2,1,0:T(8,128)(2,1)}), bf16[32,2,64,512]{3,2,1,0:T(8,128)(2,1)}, u32[]{:S(2)}, u32[]{:S(2)}) %all-to-all-start) | async-done | bytes 4194336 | tf_op jit(solution)/shard_map/all_to_all | solution.py:126
  421.2 185.9 %while.19 = (s32[]{:T(128)}, f32[256,1,128]{0,2,1:T(8,128)S(1)}, f32[256,1,128]{0,2,1:T(8,128)S(1)}, bf16[8,8,64,512]{3,2,1,0:T(8,128)(2,1)}, bf16[8,8,64,128]{3...) while((s32[]{:T(128)}, f32[256,1,128]{0,2,1:T(8,128)S(1)}, ...), condition=%wide.region_9.10_spmd.clone, body=%wide.region_1.9_spmd.clone.sunk | while | flops 851605504 | bytes 65064360 | solution.py:171
  422.2 2.1 constant_dynamic-slice_fusion.3
  445.5 2.1 constant_dynamic-slice_fusion.3
  468.7 2.1 constant_dynamic-slice_fusion.3
  491.9 2.1 constant_dynamic-slice_fusion.3
  515.2 2.1 constant_dynamic-slice_fusion.3
  538.4 2.1 constant_dynamic-slice_fusion.3
  561.6 2.1 constant_dynamic-slice_fusion.3
  584.9 2.1 constant_dynamic-slice_fusion.3
  607.1 6.5 copy.159
  613.6 103.7 %all_to_all.35 = bf16[32,2,64,512]{3,1,2,0:T(2,128)(2,1)S(1)} all-to-all(bf16[32,2,64,512]{3,1,2,0:T(2,128)(2,1)S(1)} %copy.159), channel_id=1, replica_groups=mesh['dom'=32,'tp'=8] {'dom'}, dimensions={0} | all-to-all | bytes 8388608 | tf_op jit(solution)/shard_map/all_to_all | solution.py:173
  717.4 2.4 bitcast_convert_fusion.1
  719.8 9.5 %fusion.58 = bf16[4096,512]{0,1:T(8,128)(2,1)} fusion(bf16[14,64,4096]{2,1,0:T(8,128)(2,1)} %all-gather.3.cloned.1.call-done, bf16[14,64,512]{2,0,1:T(8,128)(2,1)S(1)} %bitcast_convert_fusion.1), kind=kOutput, calls=%fused_computation.77 | convolution fusion | flops 3760193536 | bytes 12451840 | tf_op jit(solution)/shard_map/tc,tq->cq/dot_general | solution.py:203
  729.3 6.5 copy.184
  739.0 3.9 all-to-all-start.5
  742.9 2.1 copy.164
  745.0 27.9 %all-to-all-done.5 = bf16[32,2,64,128]{3,1,2,0:T(2,128)(2,1)S(1)} async-done(((bf16[32,2,64,128]{3,1,2,0:T(2,128)(2,1)}), bf16[32,2,64,128]{3,1,2,0:T(2,128)(2,1)S(1)}, u32[]{:S(2)}, u32[]{:S(2)}) %all-to-all-start.5) | async-done | bytes 1048608 | tf_op jit(solution)/shard_map/all_to_all | solution.py:180
  772.9 4.0 all-to-all-start.6
  779.8 29.1 %all-to-all-done.6 = bf16[32,2,64,128]{3,1,2,0:T(2,128)(2,1)S(1)} async-done(((bf16[32,2,64,128]{3,1,2,0:T(2,128)(2,1)}), bf16[32,2,64,128]{3,1,2,0:T(2,128)(2,1)S(1)}, u32[]{:S(2)}, u32[]{:S(2)}) %all-to-all-start.6) | async-done | bytes 1048608 | tf_op jit(solution)/shard_map/all_to_all | solution.py:187
  810.4 59.2 %reduce-scatter.4.cloned.1.call-done = bf16[128,512]{1,0:T(8,128)(2,1)} async-done(((bf16[4096,512]{1,0:T(8,128)(2,1)}), bf16[128,512]{1,0:T(8,128)(2,1)}) %reduce-scatter.4.cloned.1.call-update) | async-done | bytes 131088
  (393 shorter events, 186.6 us)
Async XLA Ops:
  7.2 17.7 %copy-start.13 = (bf16[14,64,128]{2,1,0:T(8,128)(2,1)S(1)}, bf16[14,64,128]{2,1,0:T(8,128)(2,1)}, u32[]{:S(2)}) copy-start(bf16[14,64,128]{2,1,0:T(8,128)(2,1)} %param.13) | copy-start | bytes 688132
  7.2 116.9 %all-gather.5.cloned.1.call-start = ((), (), s32[]{:S(2)}) async-start(), calls=%async_computation.9 | async-start | bytes 4325376 | tf_op jit(solution)/shard_map/all_gather | solution.py:96
  7.9 294.4 %all-gather.3.cloned.1.call-start = ((), (), s32[]{:S(2)}) async-start(), calls=%async_computation.8 | async-start | bytes 8257536 | tf_op jit(solution)/shard_map/all_gather | solution.py:86
  13.3 50.7 %copy-start.12 = (bf16[14,64,512]{2,1,0:T(8,128)(2,1)S(1)}, bf16[14,64,512]{2,1,0:T(8,128)(2,1)}, u32[]{:S(2)}) copy-start(bf16[14,64,512]{2,1,0:T(8,128)(2,1)} %param.19) | copy-start | bytes 2752516
  13.3 50.7 %copy-start.14 = (f32[14]{0:T(128)S(1)}, f32[14]{0:T(128)}, u32[]{:S(2)}) copy-start(f32[14]{0:T(128)} %param.18) | copy-start | bytes 172
  13.3 46.0 %all-to-all-start.3 = ((bf16[32,2,64,128]{3,2,1,0:T(8,128)(2,1)}), bf16[32,2,64,128]{3,2,1,0:T(8,128)(2,1)S(1)}, u32[]{:S(2)}, u32[]{:S(2)}) async-start(bf16[32,2,64,128]{3,2,1,0:T(8,128)(2,1)} %copy.158), calls=%async_computation.3 | async-start | bytes 2097152 | tf_op jit(solution)/shard_map/all_to_all | solution.py:129
  59.3 37.8 %all-to-all-start.1 = ((bf16[32,2,64,128]{3,2,1,0:T(8,128)(2,1)}), bf16[32,2,64,128]{3,2,1,0:T(8,128)(2,1)}, u32[]{:S(2)}, u32[]{:S(2)}) async-start(bf16[32,2,64,128]{3,2,1,0:T(8,128)(2,1)} %copy.154), calls=%async_computation.1 | async-start | bytes 2097152 | tf_op jit(solution)/shard_map/all_to_all | solution.py:128
  97.1 219.2 %all-to-all-start.2 = ((bf16[32,2,64,512]{3,2,1,0:T(8,128)(2,1)}), bf16[32,2,64,512]{3,2,1,0:T(8,128)(2,1)}, u32[]{:S(2)}, u32[]{:S(2)}) async-start(bf16[32,2,64,512]{3,2,1,0:T(8,128)(2,1)} %copy.156), calls=%async_computation.2 | async-start | bytes 8388608 | tf_op jit(solution)/shard_map/all_to_all | solution.py:127
  316.3 104.9 %copy-start.7 = (bf16[1,256,128]{2,1,0:T(8,128)(2,1)S(1)}, bf16[1,256,128]{2,1,0:T(8,128)(2,1)}, u32[]{:S(2)}) copy-start(bf16[1,256,128]{2,1,0:T(8,128)(2,1)} %param.15) | copy-start | bytes 196612
  316.3 104.9 %all-to-all-start = ((bf16[32,2,64,512]{3,2,1,0:T(8,128)(2,1)}), bf16[32,2,64,512]{3,2,1,0:T(8,128)(2,1)}, u32[]{:S(2)}, u32[]{:S(2)}) async-start(bf16[32,2,64,512]{3,2,1,0:T(8,128)(2,1)} %copy.152), calls=%async_computation | async-start | bytes 8388608 | tf_op jit(solution)/shard_map/all_to_all | solution.py:126
  324.5 545.1 %reduce-scatter.4.cloned.1.call-start = ((), (), s32[]{:S(2)}) async-start(), calls=%async_computation.10 | async-start | bytes 4325376
  435.7 3.5 copy-start.1
  435.7 5.5 copy-start.6
  439.2 4.8 copy-start.3
  459.0 3.5 copy-start.1
  459.0 5.5 copy-start.6
  462.5 4.8 copy-start.3
  482.2 5.5 copy-start.6
  485.7 4.8 copy-start.3
  505.5 5.5 copy-start.6
  508.9 4.8 copy-start.3
  528.7 5.5 copy-start.6
  532.2 4.8 copy-start.3
  551.9 5.5 copy-start.6
  555.4 4.8 copy-start.3
  575.1 5.5 copy-start.6
  578.6 4.8 copy-start.3
  598.4 5.5 copy-start.6
  601.8 4.8 copy-start.3
  735.7 7.2 copy-start.11
  739.0 33.9 %all-to-all-start.5 = ((bf16[32,2,64,128]{3,1,2,0:T(2,128)(2,1)}), bf16[32,2,64,128]{3,1,2,0:T(2,128)(2,1)S(1)}, u32[]{:S(2)}, u32[]{:S(2)}) async-start(bf16[32,2,64,128]{3,1,2,0:T(2,128)(2,1)} %copy.162), calls=%async_computation.5 | async-start | bytes 2097152 | tf_op jit(solution)/shard_map/all_to_all | solution.py:180
  772.9 36.1 %all-to-all-start.6 = ((bf16[32,2,64,128]{3,1,2,0:T(2,128)(2,1)}), bf16[32,2,64,128]{3,1,2,0:T(2,128)(2,1)S(1)}, u32[]{:S(2)}, u32[]{:S(2)}) async-start(bf16[32,2,64,128]{3,1,2,0:T(2,128)(2,1)} %copy.164), calls=%async_computation.6 | async-start | bytes 2097152 | tf_op jit(solution)/shard_map/all_to_all | solution.py:187
  (63 other events, 123.7 us)
Sparse Core Ops, SparseCore 0:
  10.8 113.2 all-gather.4
  125.8 176.4 all-gather.2
  735.9 133.7 reduce-scatter.3
where the time goes:
time: 885 us; the launch traced here: 876 us
  waiting for transfers between devices  473 us (53%)
  matrix products  131 us (15%)
  blocking collectives  104 us (12%)
  local copies, waits for them, and re-layouts  86.7 us (10%)
  starting transfers between devices  38.1 us (4%)
  other arithmetic  27.5 us (3%)
  between operations  14.2 us (2%)
    all_gather x1, waiting for transfers between devices, local(): features = lax.all_gather(hidden_in, 'tp', axis=2, tiled=True)  178 us
    all_to_all x1, blocking collectives, local(): lax.all_to_all(out_q.reshape(owners, capacity, length, width_q), 'dom', s...  104 us
    all_to_all x1, waiting for transfers between devices, local(): lax.all_to_all(to_slots(queries), 'dom', split_axis=0, concat_axis=0, til...  96.4 us
    unnamed x4, waiting for transfers between devices  60.6 us
    all_to_all x1, waiting for transfers between devices, local(): lax.all_to_all(to_slots(segment_values), 'dom', split_axis=0, concat_axis...  32.4 us
    all_to_all x1, waiting for transfers between devices, local(): lax.all_to_all(out_v.reshape(owners, capacity, length, width_kv), 'dom',...  29.1 us
    all_to_all x1, waiting for transfers between devices, local(): lax.all_to_all(out_k.reshape(owners, capacity, length, width_kv), 'dom',...  27.9 us
    all_to_all x1, waiting for transfers between devices, local(): lax.all_to_all(to_slots(segment_keys), 'dom', split_axis=0, concat_axis=0...  27.1 us
  transfers between devices with their start and end apart: 9, of which 8 were waited for; matrix products, arithmetic and copies ran while one was open for 4% of the time, Pallas kernels for 0%

commit v1 on v0

--- a/solution.py
+++ b/solution.py
@@ -83,7 +83,9 @@
 ):
     particles_here = hidden_in.shape[0]
     length = hidden_in.shape[1]
-    features = lax.all_gather(hidden_in, "tp", axis=2, tiled=True)
+    features = jnp.concatenate(
+        lax.all_to_all(jnp.stack([hidden_in] * lax.axis_size("tp")), "tp", 0, 0), axis=2
+    )
     token_rows = features.reshape(particles_here * length, features.shape[2])
     width_q = query_weight.shape[1]
     width_kv = segment_keys.shape[2]

time: 885 us -> 855 us (0.966)
  waiting for transfers between devices: 473 us -> 397 us
  blocking collectives: 104 us -> 138 us
  local copies, waits for them, and re-layouts: 86.7 us -> 98.1 us
    all_gather x1 -> x0, waiting for transfers between devices: 178 us -> none  [local(): features = lax.all_gather(hidden_in, 'tp', axis=2, tiled=True)]
    all_to_all x1, waiting for transfers between devices: 0.01 us -> 65.2 us  [local(): lax.all_to_all(to_slots(scaled), 'dom', split_axis=0, concat_axis=0, tile...]
    all_to_all x1, waiting for transfers between devices: 27.1 us -> 89.7 us  [local(): lax.all_to_all(jnp.stack([hidden_in] * lax.axis_size('tp')), 'tp', 0, 0)]
    all_to_all x0 -> x1, blocking collectives: none -> 33.8 us  [local(): lax.all_to_all(to_slots(segment_keys), 'dom', split_axis=0, concat_axis=0...]
    all_gather x1, waiting for transfers between devices: 21.5 us -> 1.8 us  [local(): lax.all_gather(query_weight, 'dom', axis=0, tiled=True)]
    another operation x16 -> x17, local copies, waits for them, and re-layouts: 16.7 us -> 20.9 us
    unnamed x4 -> x3, waiting for transfers between devices: 60.6 us -> 58.1 us
  transfers between devices with their start and end apart: 9 -> 8, of which waited for: 8 -> 8; matrix products, arithmetic and copies ran while one was open for 4% -> 5% of each run, Pallas kernels for 0% -> 0%
where the time goes in v1:
time: 855 us; the launch traced here: 846 us
  waiting for transfers between devices  397 us (46%)
  blocking collectives  138 us (16%)
  matrix products  130 us (15%)
  local copies, waits for them, and re-layouts  98.1 us (11%)
  starting transfers between devices  38.9 us (5%)
  other arithmetic  27.4 us (3%)
  between operations  14.4 us (2%)
    all_to_all x1, blocking collectives, local(): lax.all_to_all(out_q.reshape(owners, capacity, length, width_q), 'dom', s...  104 us
    all_to_all x1, waiting for transfers between devices, local(): lax.all_to_all(to_slots(queries), 'dom', split_axis=0, concat_axis=0, til...  96.6 us
    all_to_all x1, waiting for transfers between devices, local(): lax.all_to_all(jnp.stack([hidden_in] * lax.axis_size('tp')), 'tp', 0, 0)  89.7 us
    all_to_all x1, waiting for transfers between devices, local(): lax.all_to_all(to_slots(scaled), 'dom', split_axis=0, concat_axis=0, tile...  65.2 us
    unnamed x3, waiting for transfers between devices  58.1 us
    all_to_all x1, blocking collectives, local(): lax.all_to_all(to_slots(segment_keys), 'dom', split_axis=0, concat_axis=0...  33.8 us
    all_to_all x1, waiting for transfers between devices, local(): lax.all_to_all(out_v.reshape(owners, capacity, length, width_kv), 'dom',...  29.1 us
    all_to_all x1, waiting for transfers between devices, local(): lax.all_to_all(to_slots(segment_values), 'dom', split_axis=0, concat_axis...  29 us
  transfers between devices with their start and end apart: 8, of which 8 were waited for; matrix products, arithmetic and copies ran while one was open for 5% of the time, Pallas kernels for 0%

profile of v1, /device:TPU:2, one launch (start us, length us, event | category | flops | bytes accessed | tf_op | source)
XLA Modules:
  0.0 845.8 jit_solution(2044981689406239501)
XLA Ops:
  11.8 11.7 %all-to-all-start.4 = ((bf16[32,2,64,128]{3,2,1,0:T(8,128)(2,1)}), bf16[32,2,64,128]{3,2,1,0:T(8,128)(2,1)}, u32[]{:S(2)}, u32[]{:S(2)}) async-start(bf16[32,2,64,128]{3,2,1,0:T(8,128)(2,1)} %copy.103), calls=%async_computation.4 | async-start | bytes 2097152 | tf_op jit(solution)/shard_map/all_to_all | solution.py:131
  24.5 29.0 %all-to-all-done.4 = bf16[32,2,64,128]{3,2,1,0:T(8,128)(2,1)} async-done(((bf16[32,2,64,128]{3,2,1,0:T(8,128)(2,1)}), bf16[32,2,64,128]{3,2,1,0:T(8,128)(2,1)}, u32[]{:S(2)}, u32[]{:S(2)}) %all-to-all-start.4) | async-done | bytes 1048608 | tf_op jit(solution)/shard_map/all_to_all | solution.py:131
  53.5 33.8 %all_to_all.40 = bf16[32,2,64,128]{3,2,1,0:T(8,128)(2,1)} all-to-all(bf16[32,2,64,128]{3,2,1,0:T(8,128)(2,1)S(1)} %copy.99), channel_id=1, replica_groups=mesh['dom'=32,'tp'=8] {'dom'}, dimensions={0} | all-to-all | bytes 2097152 | tf_op jit(solution)/shard_map/all_to_all | solution.py:130
  87.3 3.9 stack.2
  91.2 5.4 all-to-all-start
  99.0 4.4 copy.101
  103.4 89.7 %all-to-all-done = bf16[8,14,64,512]{3,2,1,0:T(8,128)(2,1)} async-done(((bf16[8,14,64,512]{3,2,1,0:T(8,128)(2,1)}), bf16[8,14,64,512]{3,2,1,0:T(8,128)(2,1)}, u32[]{:S(2)}, u32[]{:S(2)}) %all-to-all-start) | async-done | bytes 7340064 | tf_op jit(solution)/shard_map/all_to_all | solution.py:87
  193.0 7.4 all-to-all-start.3
  200.4 8.1 copy.95
  208.5 7.8 copy.131
  218.2 8.2 convolution_convert_fusion.5
  227.8 4.4 copy.97
  232.1 65.2 %all-to-all-done.3 = bf16[32,2,64,512]{3,2,1,0:T(8,128)(2,1)} async-done(((bf16[32,2,64,512]{3,2,1,0:T(8,128)(2,1)}), bf16[32,2,64,512]{3,2,1,0:T(8,128)(2,1)}, u32[]{:S(2)}, u32[]{:S(2)}) %all-to-all-start.3) | async-done | bytes 4194336 | tf_op jit(solution)/shard_map/all_to_all | solution.py:129
  297.3 6.4 all-to-all-start.1
  303.8 96.6 %all-to-all-done.1 = bf16[32,2,64,512]{3,2,1,0:T(8,128)(2,1)} async-done(((bf16[32,2,64,512]{3,2,1,0:T(8,128)(2,1)}), bf16[32,2,64,512]{3,2,1,0:T(8,128)(2,1)}, u32[]{:S(2)}, u32[]{:S(2)}) %all-to-all-start.1) | async-done | bytes 4194336 | tf_op jit(solution)/shard_map/all_to_all | solution.py:128
  400.4 177.5 %while.19 = (s32[]{:T(128)}, f32[256,1,128]{0,2,1:T(8,128)S(1)}, f32[256,1,128]{0,2,1:T(8,128)S(1)}, bf16[8,8,64,512]{3,2,1,0:T(8,128)(2,1)}, bf16[8,8,64,128]{3...) while((s32[]{:T(128)}, f32[256,1,128]{0,2,1:T(8,128)S(1)}, ...), condition=%wide.region_9.10_spmd.clone, body=%wide.region_1.9_spmd.clone.sunk | while | flops 851605504 | bytes 56675696 | solution.py:173
  400.8 2.1 constant_dynamic-slice_fusion.3
  423.0 2.1 constant_dynamic-slice_fusion.3
  445.1 2.1 constant_dynamic-slice_fusion.3
  467.2 2.1 constant_dynamic-slice_fusion.3
  489.4 2.1 constant_dynamic-slice_fusion.3
  511.5 2.1 constant_dynamic-slice_fusion.3
  577.9 6.5 copy.104
  584.5 103.7 %all_to_all.41 = bf16[32,2,64,512]{3,1,2,0:T(2,128)(2,1)S(1)} all-to-all(bf16[32,2,64,512]{3,1,2,0:T(2,128)(2,1)S(1)} %copy.104), channel_id=1, replica_groups=mesh['dom'=32,'tp'=8] {'dom'}, dimensions={0} | all-to-all | bytes 8388608 | tf_op jit(solution)/shard_map/all_to_all | solution.py:175
  688.2 2.4 bitcast_convert_fusion
  691.1 9.2 %fusion.58 = bf16[4096,512]{0,1:T(8,128)(2,1)} fusion(bf16[896,512]{1,0:T(8,128)(2,1)S(1)} %bitcast.279, bf16[896,4096]{1,0:T(8,128)(2,1)} %bitcast.273), kind=kOutput, calls=%fused_computation.77 | convolution fusion | flops 3760193536 | bytes 12451840 | tf_op jit(solution)/shard_map/tc,tq->cq/dot_general | solution.py:205
  700.3 6.5 copy.129
  710.0 3.9 all-to-all-start.6
  716.1 27.9 %all-to-all-done.6 = bf16[32,2,64,128]{3,1,2,0:T(2,128)(2,1)S(1)} async-done(((bf16[32,2,64,128]{3,1,2,0:T(2,128)(2,1)}), bf16[32,2,64,128]{3,1,2,0:T(2,128)(2,1)S(1)}, u32[]{:S(2)}, u32[]{:S(2)}) %all-to-all-start.6) | async-done | bytes 1048608 | tf_op jit(solution)/shard_map/all_to_all | solution.py:182
  744.0 3.9 all-to-all-start.7
  750.9 29.1 %all-to-all-done.7 = bf16[32,2,64,128]{3,1,2,0:T(2,128)(2,1)S(1)} async-done(((bf16[32,2,64,128]{3,1,2,0:T(2,128)(2,1)}), bf16[32,2,64,128]{3,1,2,0:T(2,128)(2,1)S(1)}, u32[]{:S(2)}, u32[]{:S(2)}) %all-to-all-start.7) | async-done | bytes 1048608 | tf_op jit(solution)/shard_map/all_to_all | solution.py:189
  781.5 57.3 %reduce-scatter.4.cloned.1.call-done = bf16[128,512]{1,0:T(8,128)(2,1)} async-done(((bf16[4096,512]{1,0:T(8,128)(2,1)}), bf16[128,512]{1,0:T(8,128)(2,1)}) %reduce-scatter.4.cloned.1.call-update) | async-done | bytes 131088
  (365 shorter events, 184.5 us)
Async XLA Ops:
  7.2 16.4 %copy-start.12 = (bf16[14,64,128]{2,1,0:T(8,128)(2,1)S(1)}, bf16[14,64,128]{2,1,0:T(8,128)(2,1)}, u32[]{:S(2)}) copy-start(bf16[14,64,128]{2,1,0:T(8,128)(2,1)} %param.13) | copy-start | bytes 688132
  11.8 75.5 %copy-start.11 = (bf16[14,64,512]{2,1,0:T(8,128)(2,1)S(1)}, bf16[14,64,512]{2,1,0:T(8,128)(2,1)}, u32[]{:S(2)}) copy-start(bf16[14,64,512]{2,1,0:T(8,128)(2,1)} %param.11) | copy-start | bytes 2752516
  11.8 41.7 %all-to-all-start.4 = ((bf16[32,2,64,128]{3,2,1,0:T(8,128)(2,1)}), bf16[32,2,64,128]{3,2,1,0:T(8,128)(2,1)}, u32[]{:S(2)}, u32[]{:S(2)}) async-start(bf16[32,2,64,128]{3,2,1,0:T(8,128)(2,1)} %copy.103), calls=%async_computation.4 | async-start | bytes 2097152 | tf_op jit(solution)/shard_map/all_to_all | solution.py:131
  91.2 6.1 copy-start.10
  91.2 6.1 copy-start.13
  91.2 101.8 %all-to-all-start = ((bf16[8,14,64,512]{3,2,1,0:T(8,128)(2,1)}), bf16[8,14,64,512]{3,2,1,0:T(8,128)(2,1)}, u32[]{:S(2)}, u32[]{:S(2)}) async-start(bf16[8,14,64,512]{3,2,1,0:T(8,128)(2,1)} %stack.2), calls=%async_computation | async-start | bytes 14680064 | tf_op jit(solution)/shard_map/all_to_all | solution.py:87
  96.6 121.6 %all-gather.2.cloned.1.call-start = ((), (), s32[]{:S(2)}) async-start(), calls=%async_computation.9 | async-start | bytes 4325376 | tf_op jit(solution)/shard_map/all_gather | solution.py:98
  193.0 104.3 %all-to-all-start.3 = ((bf16[32,2,64,512]{3,2,1,0:T(8,128)(2,1)}), bf16[32,2,64,512]{3,2,1,0:T(8,128)(2,1)}, u32[]{:S(2)}, u32[]{:S(2)}) async-start(bf16[32,2,64,512]{3,2,1,0:T(8,128)(2,1)} %copy.101), calls=%async_computation.3 | async-start | bytes 8388608 | tf_op jit(solution)/shard_map/all_to_all | solution.py:129
  232.1 168.3 %copy-start.7 = (bf16[1,256,128]{2,1,0:T(8,128)(2,1)S(1)}, bf16[1,256,128]{2,1,0:T(8,128)(2,1)}, u32[]{:S(2)}) copy-start(bf16[1,256,128]{2,1,0:T(8,128)(2,1)} %param.15) | copy-start | bytes 196612
  297.3 103.1 %all-to-all-start.1 = ((bf16[32,2,64,512]{3,2,1,0:T(8,128)(2,1)}), bf16[32,2,64,512]{3,2,1,0:T(8,128)(2,1)}, u32[]{:S(2)}, u32[]{:S(2)}) async-start(bf16[32,2,64,512]{3,2,1,0:T(8,128)(2,1)} %copy.97), calls=%async_computation.1 | async-start | bytes 8388608 | tf_op jit(solution)/shard_map/all_to_all | solution.py:128
  303.7 535.1 %reduce-scatter.4.cloned.1.call-start = ((), (), s32[]{:S(2)}) async-start(), calls=%async_computation.10 | async-start | bytes 4325376
  414.3 3.5 copy-start.1
  414.3 5.5 copy-start.6
  417.8 4.7 copy-start.3
  436.5 5.5 copy-start.6
  440.0 4.7 copy-start.3
  458.7 5.5 copy-start.6
  462.1 4.7 copy-start.3
  480.8 5.5 copy-start.6
  484.2 4.7 copy-start.3
  502.9 3.5 copy-start.1
  502.9 5.5 copy-start.6
  506.4 4.7 copy-start.3
  525.1 5.5 copy-start.6
  528.5 4.7 copy-start.3
  547.2 5.5 copy-start.6
  550.7 4.7 copy-start.3
  569.3 5.5 copy-start.6
  572.8 4.7 copy-start.3
  706.8 7.2 copy-start.9
  710.0 33.9 %all-to-all-start.6 = ((bf16[32,2,64,128]{3,1,2,0:T(2,128)(2,1)}), bf16[32,2,64,128]{3,1,2,0:T(2,128)(2,1)S(1)}, u32[]{:S(2)}, u32[]{:S(2)}) async-start(bf16[32,2,64,128]{3,1,2,0:T(2,128)(2,1)} %copy.107), calls=%async_computation.6 | async-start | bytes 2097152 | tf_op jit(solution)/shard_map/all_to_all | solution.py:182
  744.0 36.0 %all-to-all-start.7 = ((bf16[32,2,64,128]{3,1,2,0:T(2,128)(2,1)}), bf16[32,2,64,128]{3,1,2,0:T(2,128)(2,1)S(1)}, u32[]{:S(2)}, u32[]{:S(2)}) async-start(bf16[32,2,64,128]{3,1,2,0:T(2,128)(2,1)} %copy.109), calls=%async_computation.7 | async-start | bytes 2097152 | tf_op jit(solution)/shard_map/all_to_all | solution.py:189
  (47 other events, 98.4 us)
Sparse Core Ops, SparseCore 0:
  100.2 117.9 all-gather.1
  706.9 131.8 reduce-scatter.3
